TPU v7x, 32 devices: a whole 2x2x4 slice. The times are simulated.
32 devices in a mesh: groups: 2 (over y), dp: 4 (over z), mp: 4 (over x, core).
Axes of the slice: x: 2, y: 2, z: 4, core: 2. Of those that a mesh axis runs over, the one named last changes fastest.
Arguments:
- latents: bfloat16 [256, 640, 64], P(('groups', 'dp'), 'mp'), parts along dimension 0
- modulation: bfloat16 [256, 2, 640], P(('groups', 'dp'), None, 'mp'), parts along dimension 0, may hold values from -3 to 3
- first_kernel: bfloat16 [640, 9, 640], P('dp', None, 'mp'), may hold values from -0.078125 to 0.078125
- second_kernel: bfloat16 [640, 9, 640], P('dp', None, 'mp'), may hold values from -0.078125 to 0.078125
- encoder_cache: bfloat16 [336, 1280, 128], P(('groups', 'dp'), 'mp'), parts along dimension 0
- query_weight: bfloat16 [640, 640], P('dp'), may hold values from -0.25 to 0.25
- output_weight: bfloat16 [640, 640], P('dp'), may hold values from -0.25 to 0.25
- kept_prompt_list: int32 [256], P('groups'), parts along dimension 0, may hold values from 0 to 167, as said below
- destination: int32 [256], P('groups'), parts along dimension 0, may hold values from 0 to 3, as said below
- lengths: int32 [336], P('groups'), parts along dimension 0, may hold values from 1 to 128, 10752 in all
Outputs:
- level_out: bfloat16 [256, 640, 64], P(('groups', 'dp'), 'mp'), parts along dimension 0
There are 2 independent parts, one for each index of `groups`. A program takes and returns all parts, laid end to end along the dimension named above; an argument that names none is the same for every part. Nothing has to cross between parts.
Inputs may be any that keep to these rules, and one draw needn't show every extreme that they name: `kept_prompt_list`: entries o * 32 to o * 32 + 31 belong to owner o: distinct ids of its prompts o * 42 to o * 42 + 41. `destination`: names the shard of each survivor; every shard receives exactly 32 survivors, one owner sends at most 16 survivors to one shard, and every owner sends exactly 16 to some shard.
All inputs are finite; a program needn't handle non-finite values.
Results may differ from a plain program's by a relative error of at most 0.0055.
Values may be sent and summed in bfloat16 or wider, within the bound.
No kernel may reach another device: no remote copies, remote signals or barrier semaphores. Data moves between devices by JAX's collectives and lax.ppermute only.
A program may use at most 64 MiB of HBM per device.

v0:
```python
import jax
import jax.numpy as jnp
from jax import lax
from jax.sharding import PartitionSpec as P

C = 640
GROUPS = 32
HEAD = 64
SIDE = 8
EPSILON = 1e-05
MASKED = -1e30


def norm_groups(values, group_width):
    field_shape = values.shape
    grouped = values.reshape(
        field_shape[0], field_shape[1] // group_width, group_width, field_shape[2]
    )
    center = grouped - jnp.mean(grouped, axis=(2, 3), keepdims=True)
    spread = jnp.mean(center * center, axis=(2, 3), keepdims=True)
    return (center * lax.rsqrt(spread + EPSILON)).reshape(field_shape)


def gather_channels(field):
    return lax.all_gather(field, "mp", axis=1, tiled=True)


def pair_gather_channels(field):
    across = lax.ppermute(field, "mp", [(i, i ^ 2) for i in range(4)])
    beside = lax.ppermute(field, "mp", [(i, i ^ 1) for i in range(4)])
    relayed = lax.ppermute(across, "mp", [(i, i ^ 1) for i in range(4)])
    return jnp.concatenate([field, beside, across, relayed], axis=1)


def shift_parts(shard, count):
    parts = [shard]
    for step in range(1, count):
        parts.append(lax.ppermute(shard, "dp", [(i, (i + step) % count) for i in range(count)]))
    return jnp.stack(parts)


def order_rows(stacked, wanted_blocks):
    my_shard = lax.axis_index("dp")
    count = stacked.shape[0]
    picked = jnp.take(stacked, (my_shard - wanted_blocks) % count, axis=0, mode="clip")
    return picked.reshape((count * stacked.shape[1],) + stacked.shape[2:])


def gather_kernel(weight_shard):
    return lax.all_gather(weight_shard, "dp", axis=0, tiled=True)


def gather_projection(weight_shard):
    return lax.all_gather(weight_shard, "dp", axis=0, tiled=True)


def apply_kernel(full_field, kernel):
    sample_count = full_field.shape[0]
    out_width = kernel.shape[2]
    tap_images = jnp.einsum("scq,cte->steq", full_field, kernel, preferred_element_type=jnp.float32)
    tap_images = tap_images.reshape(sample_count, 9, out_width, SIDE, SIDE)
    padded = jnp.pad(tap_images, ((0, 0), (0, 0), (0, 0), (1, 1), (1, 1)))
    running = padded[:, 0, :, 0:SIDE, 0:SIDE]
    for offset in range(1, 9):
        row_shift, col_shift = (offset // 3, offset % 3)
        running = (
            running
            + padded[:, offset, :, row_shift : row_shift + SIDE, col_shift : col_shift + SIDE]
        )
    return running.reshape(sample_count, out_width, SIDE * SIDE)


def local(
    latents,
    modulation,
    first_kernel,
    second_kernel,
    encoder_cache,
    query_weight,
    output_weight,
    kept_prompt_list,
    destination,
    lengths,
):
    group_width = C // GROUPS
    dp_count = lax.axis_size("dp")
    mp_count = lax.axis_size("mp")
    my_shard = lax.axis_index("dp")
    my_column = lax.axis_index("mp")
    sample_shard_count = latents.shape[0]
    prompt_dev = encoder_cache.shape[0]
    cache_len = encoder_cache.shape[2]
    cache_width = encoder_cache.shape[1]
    cell_count = latents.shape[2]
    slot_limit = 2 * (sample_shard_count // dp_count)
    all_samples = destination.shape[0]
    owner_target = destination.reshape(dp_count, sample_shard_count)
    positions = jnp.arange(sample_shard_count, dtype=jnp.int32)
    before = positions[None, :] < positions[:, None]
    same_target = owner_target[:, :, None] == owner_target[:, None, :]
    slot_rank = jnp.sum((same_target & before[None]).astype(jnp.int32), axis=2)
    my_target = lax.dynamic_index_in_dim(owner_target, my_shard, 0, keepdims=False)
    my_rank = lax.dynamic_index_in_dim(slot_rank, my_shard, 0, keepdims=False)
    my_prompts = (
        lax.dynamic_slice_in_dim(
            kept_prompt_list, my_shard * sample_shard_count, sample_shard_count
        )
        - my_shard * prompt_dev
    )
    send_slot = my_target * slot_limit + my_rank
    slot_table = send_slot[:, None] == jnp.arange(dp_count * slot_limit, dtype=jnp.int32)[None, :]
    source_row = jnp.sum(jnp.where(slot_table, my_prompts[:, None], 0), axis=0)
    filled = jnp.any(slot_table, axis=0)
    send_rows = jnp.take(encoder_cache, source_row, axis=0)
    send_rows = jnp.where(filled[:, None, None], send_rows, jnp.zeros_like(send_rows))
    outgoing = send_rows.reshape(dp_count, slot_limit, cache_width, cache_len)
    incoming = lax.all_to_all(outgoing, "dp", split_axis=0, concat_axis=0, tiled=True)
    arriving = destination == my_shard
    arrival_pos = jnp.cumsum(arriving.astype(jnp.int32)) - 1
    selector = arriving[None, :] & (arrival_pos[None, :] == positions[:, None])
    kept_prompt = jnp.sum(
        jnp.where(selector, jnp.arange(all_samples, dtype=jnp.int32)[None, :], 0), axis=1
    )
    incoming_order_rank = jnp.sum(jnp.where(selector, slot_rank.reshape(-1)[None, :], 0), axis=1)
    prompt_ids = jnp.sum(jnp.where(selector, kept_prompt_list[None, :], 0), axis=1)
    landing_slot = kept_prompt // sample_shard_count * slot_limit + incoming_order_rank
    my_pairs = jnp.take(
        incoming.reshape(dp_count * slot_limit, cache_width, cache_len), landing_slot, axis=0
    )
    prompt_hits = prompt_ids[:, None] == jnp.arange(lengths.shape[0], dtype=jnp.int32)[None, :]
    my_lengths = jnp.sum(jnp.where(prompt_hits, lengths[None, :], 0), axis=1)
    fast = dp_count == 4 and mp_count == 4
    weight_shards = (first_kernel, second_kernel, query_weight, output_weight)
    if fast:
        block_ids = jnp.arange(dp_count, dtype=jnp.int32)
        channel_blocks = jnp.bitwise_xor(block_ids, my_column)
        full_weights = (
            order_rows(shift_parts(first_kernel, dp_count), channel_blocks),
            order_rows(shift_parts(second_kernel, dp_count), channel_blocks),
            order_rows(shift_parts(query_weight, dp_count), block_ids),
            order_rows(shift_parts(output_weight, dp_count), block_ids),
        )
        spread_channels = pair_gather_channels
    else:
        full_weights = (
            gather_kernel(first_kernel),
            gather_kernel(second_kernel),
            gather_projection(query_weight),
            gather_projection(output_weight),
        )
        spread_channels = gather_channels
    start_field = latents.astype(jnp.float32)
    activated = jax.nn.silu(norm_groups(start_field, group_width)).astype(jnp.bfloat16)
    first_in = spread_channels(activated)

    def convolve(full_field, which_weight):
        return apply_kernel(full_field, full_weights[which_weight])

    def project(field_rows, which_weight):
        full_weight = full_weights[which_weight]
        return jnp.einsum(
            "scq,ce->seq", field_rows, full_weight, preferred_element_type=jnp.float32
        )

    first_out = convolve(first_in, 0)
    scale_term = modulation[:, 0, :].astype(jnp.float32)[:, :, None]
    shift_term = modulation[:, 1, :].astype(jnp.float32)[:, :, None]
    modulated = jax.nn.silu(
        norm_groups(first_out, group_width) * (1.0 + scale_term) + shift_term
    ).astype(jnp.bfloat16)
    second_in = spread_channels(modulated)
    residual = start_field + convolve(second_in, 1)
    normed_out = norm_groups(residual, group_width).astype(jnp.bfloat16)
    local_samples = sample_shard_count // mp_count
    query_cells, pair_heads = (
        lax.all_to_all(normed_out, "mp", split_axis=0, concat_axis=1, tiled=True),
        lax.all_to_all(my_pairs, "mp", split_axis=0, concat_axis=1, tiled=True),
    )
    total_width = query_cells.shape[1]
    head_count = total_width // HEAD
    queries = project(query_cells, 2).astype(jnp.bfloat16)
    queries = queries.reshape(local_samples, head_count, HEAD, cell_count)
    heads_of_keys = pair_heads[:, :total_width, :].reshape(
        local_samples, head_count, HEAD, cache_len
    )
    value_heads = pair_heads[:, total_width:, :].reshape(local_samples, head_count, HEAD, cache_len)
    scores = jnp.einsum(
        "shdq,shdk->shqk", queries, heads_of_keys, preferred_element_type=jnp.float32
    ) * HEAD ** (-0.5)
    local_lengths = lax.dynamic_slice_in_dim(my_lengths, my_column * local_samples, local_samples)
    visible = (
        jnp.arange(cache_len, dtype=jnp.int32)[None, None, None, :]
        < local_lengths[:, None, None, None]
    )
    scores = jnp.where(visible, scores, MASKED)
    row_peak = jnp.max(scores, axis=3, keepdims=True)
    exponent = jnp.exp(scores - row_peak)
    attention = (exponent / jnp.sum(exponent, axis=3, keepdims=True)).astype(jnp.bfloat16)
    context = jnp.einsum(
        "shqk,shdk->shdq", attention, value_heads, preferred_element_type=jnp.float32
    ).astype(jnp.bfloat16)
    attended = project(context.reshape(local_samples, total_width, cell_count), 3).astype(
        jnp.bfloat16
    )
    returned = lax.all_to_all(attended, "mp", split_axis=1, concat_axis=0, tiled=True)
    final_field = residual + returned.astype(jnp.float32)
    return final_field.astype(jnp.bfloat16)


def solution(mesh):
    in_specs = (
        P(("groups", "dp"), "mp", None),
        P(("groups", "dp"), None, "mp"),
        P("dp", None, "mp"),
        P("dp", None, "mp"),
        P(("groups", "dp"), "mp", None),
        P("dp", None),
        P("dp", None),
        P("groups"),
        P("groups"),
        P("groups"),
    )
    out_specs = P(("groups", "dp"), "mp", None)
    return jax.shard_map(local, mesh=mesh, in_specs=in_specs, out_specs=out_specs, check_vma=False)
```

profile of v0, /device:TPU:8, one launch (start us, length us, event | category | flops | bytes accessed | tf_op | source)
XLA Modules:
  0.0 435.4 jit_solution(7232761819546583479)
XLA Ops:
  2.3 3.5 gather_fusion.3
  5.8 5.5 %select_select_fusion = bf16[4,16,320,128]{3,2,1,0:T(8,128)(2,1)} fusion(bf16[4,16,320,128]{3,2,1,0:T(8,128)(2,1)} %bitcast.138, pred[4,16]{1,0:T(4,128)(4,1)S(1)} %compare_and_fusion, pred[4,16]{1,0:T(4,128)(4,1)S(1)} %broadcast_in_dim.133), kind=kLoop, calls=%fused_computation.25 | loop fusion | flops 5242880 | bytes 10485888 | tf_op jit(solution)/shard_map/jit(_where)/select_n | solution.py:115
  11.3 5.4 %all-to-all-start = ((bf16[4,16,320,128]{3,2,1,0:T(8,128)(2,1)}), bf16[4,16,320,128]{3,2,1,0:T(8,128)(2,1)}, u32[]{:S(2)}, u32[]{:S(2)}) async-start(bf16[4,16,320,128]{3,2,1,0:T(8,128)(2,1)} %select_select_fusion), calls=%async_computation | async-start | bytes 10485760 | tf_op jit(solution)/shard_map/all_to_all | solution.py:117
  23.9 2.0 collective-permute-start.5
  26.0 18.9 %collective-permute-done.7 = bf16[32,160,64]{1,2,0:T(8,128)(2,1)} collective-permute-done((bf16[32,160,64]{1,2,0:T(8,128)(2,1)}, bf16[32,160,64]{1,2,0:T(8,128)(2,1)}, u32[]{:S(2)}, u32[]{:S(2)}) %collective-permute-start.7) | collective-permute-done | bytes 655392 | tf_op jit(solution)/shard_map/ppermute | solution.py:29
  44.9 132.9 %collective-permute-done.3 = bf16[160,9,160]{2,0,1:T(8,128)(2,1)S(1)} collective-permute-done((bf16[160,9,160]{2,0,1:T(8,128)(2,1)S(1)}, bf16[160,9,160]{2,0,1:T(8,128)(2,1)S(1)}, u32[]{:S(2)}, u32[]{:S(2)}) %collective-permute-start.3) | collective-permute-done | bytes 460832 | tf_op jit(solution)/shard_map/ppermute | solution.py:38
  177.9 14.6 %collective-permute-done.4 = bf16[160,9,160]{2,0,1:T(8,128)(2,1)S(1)} collective-permute-done((bf16[160,9,160]{2,0,1:T(8,128)(2,1)S(1)}, bf16[160,9,160]{2,0,1:T(8,128)(2,1)S(1)}, u32[]{:S(2)}, u32[]{:S(2)}) %collective-permute-start.4) | collective-permute-done | bytes 460832 | tf_op jit(solution)/shard_map/ppermute | solution.py:38
  192.5 2.0 collective-permute-done.5
  195.4 2.2 pad_maximum_fusion.1
  197.6 2.4 gather_fusion.1
  200.0 6.2 %copy.50 = bf16[4,160,9,160]{1,0,3,2:T(4,128)(2,1)S(1)} copy(bf16[4,160,9,160]{3,1,2,0:T(8,128)(2,1)} %gather_fusion.1) | data formatting | bytes 3686400 | tf_op jit(solution)/shard_map/jit(_take)/gather | solution.py:45
  206.2 3.0 reshape.482
  209.2 11.4 %convolution_bitcast_fusion.1 = f32[32,9,160,8,8]{2,4,3,0,1:T(8,128)S(1)} fusion(bf16[32,160,64]{1,2,0:T(8,128)(2,1)} %collective-permute-done.8, bf16[32,160,64]{1,2,0:T(8,128)(2,1)} %collective-permute-done.7, bf16[32,160,64]{1,2,0:T(8,128)(2,1)} %collective-permute-done.6, bf16[32,160,64]{1,2,0:T(8,128)(2,1)} %fusion.36, ...), kind=kOutput, calls=%fused_computation.24 | convolution fusion | flops 3785359360 | bytes 16261120 | tf_op jit(solution)/shard_map/scq,cte->steq/dot_general | solution.py:60
  220.6 2.3 fusion.75
  224.1 1.7 multiply_convert_fusion.1
  229.1 2.0 collective-permute-start.2
  231.5 18.9 %collective-permute-done.10 = bf16[32,160,64]{1,2,0:T(8,128)(2,1)} collective-permute-done((bf16[32,160,64]{1,2,0:T(8,128)(2,1)}, bf16[32,160,64]{1,2,0:T(8,128)(2,1)}, u32[]{:S(2)}, u32[]{:S(2)}) %collective-permute-start.10) | collective-permute-done | bytes 655392 | tf_op jit(solution)/shard_map/ppermute | solution.py:29
  250.7 25.1 %collective-permute-done = bf16[160,9,160]{2,0,1:T(8,128)(2,1)S(1)} collective-permute-done((bf16[160,9,160]{2,0,1:T(8,128)(2,1)S(1)}, bf16[160,9,160]{2,0,1:T(8,128)(2,1)S(1)}, u32[]{:S(2)}, u32[]{:S(2)}) %collective-permute-start) | collective-permute-done | bytes 460832 | tf_op jit(solution)/shard_map/ppermute | solution.py:38
  275.8 13.9 %collective-permute-done.1 = bf16[160,9,160]{2,0,1:T(8,128)(2,1)S(1)} collective-permute-done((bf16[160,9,160]{2,0,1:T(8,128)(2,1)S(1)}, bf16[160,9,160]{2,0,1:T(8,128)(2,1)S(1)}, u32[]{:S(2)}, u32[]{:S(2)}) %collective-permute-start.1) | collective-permute-done | bytes 460832 | tf_op jit(solution)/shard_map/ppermute | solution.py:38
  289.7 2.2 collective-permute-done.2
  292.0 2.2 pad_maximum_fusion
  294.1 2.4 gather_fusion
  296.6 6.2 %copy.49 = bf16[4,160,9,160]{1,0,3,2:T(4,128)(2,1)S(1)} copy(bf16[4,160,9,160]{3,1,2,0:T(8,128)(2,1)} %gather_fusion) | data formatting | bytes 3686400 | tf_op jit(solution)/shard_map/jit(_take)/gather | solution.py:45
  302.8 3.0 reshape.484
  305.7 11.5 %convolution_bitcast_fusion = f32[32,9,160,8,8]{2,4,3,0,1:T(8,128)S(1)} fusion(bf16[32,160,64]{1,2,0:T(8,128)(2,1)} %collective-permute-done.11, bf16[32,160,64]{1,2,0:T(8,128)(2,1)} %collective-permute-done.10, bf16[32,160,64]{1,2,0:T(8,128)(2,1)} %collective-permute-done.9, bf16[32,160,64]{1,2,0:T(8,128)(2,1)} %multiply_convert_fusion.1, ...), kind=kOutput, calls=%fused_computation.23 | convolution fusion | flops 3785359360 | bytes 16261120 | tf_op jit(solution)/shard_map/scq,cte->steq/dot_general | solution.py:60
  317.2 2.4 fusion.74
  322.2 4.3 all-to-all-start.2
  326.5 3.5 gather_fusion.4
  330.1 1.8 broadcast_select_fusion
  331.9 9.1 %all-to-all-done.2 = bf16[32,160,64]{1,2,0:T(8,128)(2,1)} async-done(((bf16[32,160,64]{1,2,0:T(8,128)(2,1)}), bf16[32,160,64]{1,2,0:T(8,128)(2,1)}, u32[]{:S(2)}, u32[]{:S(2)}) %all-to-all-start.2) | async-done | bytes 655392 | tf_op jit(solution)/shard_map/all_to_all | solution.py:176
  341.0 3.7 all-to-all-start.1
  344.7 2.0 collective-permute-start.16
  346.8 1.9 collective-permute-start.17
  348.8 2.7 collective-permute-start.13
  354.3 9.2 %collective-permute-done.16 = bf16[160,640]{1,0:T(8,128)(2,1)S(1)} collective-permute-done((bf16[160,640]{1,0:T(8,128)(2,1)S(1)}, bf16[160,640]{1,0:T(8,128)(2,1)S(1)}, u32[]{:S(2)}, u32[]{:S(2)}) %collective-permute-start.16) | collective-permute-done | bytes 204832 | tf_op jit(solution)/shard_map/ppermute | solution.py:38
  363.4 11.0 %collective-permute-done.17 = bf16[160,640]{1,0:T(8,128)(2,1)S(1)} collective-permute-done((bf16[160,640]{1,0:T(8,128)(2,1)S(1)}, bf16[160,640]{1,0:T(8,128)(2,1)S(1)}, u32[]{:S(2)}, u32[]{:S(2)}) %collective-permute-start.17) | collective-permute-done | bytes 204832 | tf_op jit(solution)/shard_map/ppermute | solution.py:38
  378.0 2.8 collective-permute-done.13
  380.8 2.5 collective-permute-done.14
  383.3 2.2 pad_maximum_fusion.3
  385.5 1.8 gather_fusion.2
  387.4 3.1 fusion.50
  390.5 2.3 copy.56
  394.7 2.1 fusion.80
  396.8 1.9 fusion.79
  398.7 11.1 %convolution_convert_fusion = bf16[8,10,64,64]{3,2,1,0:T(8,128)(2,1)S(1)} fusion(bf16[8,10,64,128]{3,2,1,0:T(8,128)(2,1)} %bitcast.150, f32[8,10,64]{2,1,0:T(8,128)S(1)} %fusion.79, f32[8,10,64,128]{3,2,1,0:T(8,128)} %fusion.80, pred[8,128]{1,0:T(8,128)(4,1)S(1)} %iota_compare_fusion.4), kind=kOutput, calls=%fused_computation.87 | convolution fusion | flops 87495808 | bytes 4609024 | tf_op jit(solution)/shard_map/shqk,shdk->shdq/dot_general | solution.py:199
  413.7 13.0 %all_to_all.47 = bf16[4,2,40960]{2,1,0:T(2,128)(2,1)S(1)} all-to-all(bf16[4,2,40960]{2,1,0:T(2,128)(2,1)S(1)} %reshape.493), channel_id=1, replica_groups=mesh['groups'=2,'dp'=4,'mp'=4] {'mp'}, dimensions={0} | all-to-all | bytes 1310720 | tf_op jit(solution)/shard_map/all_to_all | solution.py:205
  428.4 3.5 copy.60
  431.9 3.5 fusion.38
  (140 shorter events, 31.7 us)
Async XLA Ops:
  0.0 2.3 copy-start
  11.3 5.5 %copy-start.3 = (bf16[32,160,64]{1,2,0:T(8,128)(2,1)S(1)}, bf16[32,160,64]{1,2,0:T(8,128)(2,1)}, u32[]{:S(2)}) copy-start(bf16[32,160,64]{1,2,0:T(8,128)(2,1)} %param.10) | copy-start | bytes 1966084
  11.3 310.9 %all-to-all-start = ((bf16[4,16,320,128]{3,2,1,0:T(8,128)(2,1)}), bf16[4,16,320,128]{3,2,1,0:T(8,128)(2,1)}, u32[]{:S(2)}, u32[]{:S(2)}) async-start(bf16[4,16,320,128]{3,2,1,0:T(8,128)(2,1)} %select_select_fusion), calls=%async_computation | async-start | bytes 10485760 | tf_op jit(solution)/shard_map/all_to_all | solution.py:117
  17.3 4.3 copy-start.6
  17.3 8.7 %copy-start.17 = (bf16[32,2,160]{2,1,0:T(2,128)(2,1)S(1)}, bf16[32,2,160]{2,1,0:T(2,128)(2,1)}, u32[]{:S(2)}) copy-start(bf16[32,2,160]{2,1,0:T(2,128)(2,1)} %param.11) | copy-start | bytes 61444
  19.9 25.0 %collective-permute-start.7 = (bf16[32,160,64]{1,2,0:T(8,128)(2,1)}, bf16[32,160,64]{1,2,0:T(8,128)(2,1)}, u32[]{:S(2)}, u32[]{:S(2)}) collective-permute-start(bf16[32,160,64]{1,2,0:T(8,128)(2,1)} %fusion.36), channel_id=1, source_target_pairs={{0,2},{1,3},{2,0},{3,1},{4,6},{5,7},{6,4},{7,5},{8,10},{9,11},{10,... | collective-permute-start | bytes 1966088 | tf_op jit(solution)/shard_map/ppermute | solution.py:29
  21.5 156.3 %collective-permute-start.3 = (bf16[160,9,160]{2,0,1:T(8,128)(2,1)S(1)}, bf16[160,9,160]{2,0,1:T(8,128)(2,1)S(1)}, u32[]{:S(2)}, u32[]{:S(2)}) collective-permute-start(bf16[160,9,160]{2,0,1:T(8,128)(2,1)S(1)} %copy-done.6), channel_id=1, source_target_pairs={{0,4},{4,8},{8,12},{12,0},{1,5},{5,9},{9,13},{13,1},{2,6},{6,10},{... | collective-permute-start | bytes 1382408 | tf_op jit(solution)/shard_map/ppermute | solution.py:38
  23.0 169.5 %collective-permute-start.4 = (bf16[160,9,160]{2,0,1:T(8,128)(2,1)S(1)}, bf16[160,9,160]{2,0,1:T(8,128)(2,1)S(1)}, u32[]{:S(2)}, u32[]{:S(2)}) collective-permute-start(bf16[160,9,160]{2,0,1:T(8,128)(2,1)S(1)} %copy-done.6), channel_id=1, source_target_pairs={{0,8},{4,12},{8,0},{12,4},{1,9},{5,13},{9,1},{13,5},{2,10},{6,14},... | collective-permute-start | bytes 1382408 | tf_op jit(solution)/shard_map/ppermute | solution.py:38
  23.9 170.6 %collective-permute-start.5 = (bf16[160,9,160]{2,0,1:T(8,128)(2,1)S(1)}, bf16[160,9,160]{2,0,1:T(8,128)(2,1)S(1)}, u32[]{:S(2)}, u32[]{:S(2)}) collective-permute-start(bf16[160,9,160]{2,0,1:T(8,128)(2,1)S(1)} %copy-done.6), channel_id=1, source_target_pairs={{0,12},{4,0},{8,4},{12,8},{1,13},{5,1},{9,5},{13,9},{2,14},{6,2},{... | collective-permute-start | bytes 1382408 | tf_op jit(solution)/shard_map/ppermute | solution.py:38
  25.9 183.3 %collective-permute-start.6 = (bf16[32,160,64]{1,2,0:T(8,128)(2,1)}, bf16[32,160,64]{1,2,0:T(8,128)(2,1)}, u32[]{:S(2)}, u32[]{:S(2)}) collective-permute-start(bf16[32,160,64]{1,2,0:T(8,128)(2,1)} %fusion.36), channel_id=1, source_target_pairs={{0,1},{1,0},{2,3},{3,2},{4,5},{5,4},{6,7},{7,6},{8,9},{9,8},{10,11... | collective-permute-start | bytes 1966088 | tf_op jit(solution)/shard_map/ppermute | solution.py:30
  44.9 164.3 %collective-permute-start.8 = (bf16[32,160,64]{1,2,0:T(8,128)(2,1)}, bf16[32,160,64]{1,2,0:T(8,128)(2,1)}, u32[]{:S(2)}, u32[]{:S(2)}) collective-permute-start(bf16[32,160,64]{1,2,0:T(8,128)(2,1)} %collective-permute-done.7), channel_id=1, source_target_pairs={{0,1},{1,0},{2,3},{3,2},{4,5},{5,4},{6,7},{7,6},{8,9},{9,8},{10,11... | collective-permute-start | bytes 1966088 | tf_op jit(solution)/shard_map/ppermute | solution.py:31
  177.8 16.7 %copy-start.10 = (bf16[160,9,160]{2,0,1:T(8,128)(2,1)}, bf16[160,9,160]{2,0,1:T(8,128)(2,1)S(1)}, u32[]{:S(2)}) copy-start(bf16[160,9,160]{2,0,1:T(8,128)(2,1)S(1)} %collective-permute-done.3) | copy-start | bytes 1382404
  192.5 2.1 copy-start.11
  194.5 0.9 copy-start.12
  223.7 3.7 copy-start.7
  223.7 7.4 %copy-start.18 = (s32[128]{0:T(128)S(1)}, s32[128]{0:T(128)}, u32[]{:S(2)}) copy-start(s32[128]{0:T(128)} %param.18) | copy-start | bytes 1540
  223.7 26.9 %copy-start.19 = (s32[128]{0:T(128)S(1)}, s32[128]{0:T(128)}, u32[]{:S(2)}) copy-start(s32[128]{0:T(128)} %param.17) | copy-start | bytes 1540
  225.9 24.5 %collective-permute-start.10 = (bf16[32,160,64]{1,2,0:T(8,128)(2,1)}, bf16[32,160,64]{1,2,0:T(8,128)(2,1)}, u32[]{:S(2)}, u32[]{:S(2)}) collective-permute-start(bf16[32,160,64]{1,2,0:T(8,128)(2,1)} %multiply_convert_fusion.1), channel_id=1, source_target_pairs={{0,2},{1,3},{2,0},{3,1},{4,6},{5,7},{6,4},{7,5},{8,10},{9,11},{10,... | collective-permute-start | bytes 1966088 | tf_op jit(solution)/shard_map/ppermute | solution.py:29
  227.4 48.4 %collective-permute-start = (bf16[160,9,160]{2,0,1:T(8,128)(2,1)S(1)}, bf16[160,9,160]{2,0,1:T(8,128)(2,1)S(1)}, u32[]{:S(2)}, u32[]{:S(2)}) collective-permute-start(bf16[160,9,160]{2,0,1:T(8,128)(2,1)S(1)} %copy-done.7), channel_id=1, source_target_pairs={{0,4},{4,8},{8,12},{12,0},{1,5},{5,9},{9,13},{13,1},{2,6},{6,10},{... | collective-permute-start | bytes 1382408 | tf_op jit(solution)/shard_map/ppermute | solution.py:38
  227.4 62.3 %collective-permute-start.1 = (bf16[160,9,160]{2,0,1:T(8,128)(2,1)S(1)}, bf16[160,9,160]{2,0,1:T(8,128)(2,1)S(1)}, u32[]{:S(2)}, u32[]{:S(2)}) collective-permute-start(bf16[160,9,160]{2,0,1:T(8,128)(2,1)S(1)} %copy-done.7), channel_id=1, source_target_pairs={{0,8},{4,12},{8,0},{12,4},{1,9},{5,13},{9,1},{13,5},{2,10},{6,14},... | collective-permute-start | bytes 1382408 | tf_op jit(solution)/shard_map/ppermute | solution.py:38
  229.1 62.9 %collective-permute-start.2 = (bf16[160,9,160]{2,0,1:T(8,128)(2,1)S(1)}, bf16[160,9,160]{2,0,1:T(8,128)(2,1)}, u32[]{:S(2)}, u32[]{:S(2)}) collective-permute-start(bf16[160,9,160]{2,0,1:T(8,128)(2,1)S(1)} %copy-done.7), channel_id=1, source_target_pairs={{0,12},{4,0},{8,4},{12,8},{1,13},{5,1},{9,5},{13,9},{2,14},{6,2},{... | collective-permute-start | bytes 1382408 | tf_op jit(solution)/shard_map/ppermute | solution.py:38
  231.4 74.4 %collective-permute-start.9 = (bf16[32,160,64]{1,2,0:T(8,128)(2,1)}, bf16[32,160,64]{1,2,0:T(8,128)(2,1)}, u32[]{:S(2)}, u32[]{:S(2)}) collective-permute-start(bf16[32,160,64]{1,2,0:T(8,128)(2,1)} %multiply_convert_fusion.1), channel_id=1, source_target_pairs={{0,1},{1,0},{2,3},{3,2},{4,5},{5,4},{6,7},{7,6},{8,9},{9,8},{10,11... | collective-permute-start | bytes 1966088 | tf_op jit(solution)/shard_map/ppermute | solution.py:30
  250.4 55.4 %collective-permute-start.11 = (bf16[32,160,64]{1,2,0:T(8,128)(2,1)}, bf16[32,160,64]{1,2,0:T(8,128)(2,1)}, u32[]{:S(2)}, u32[]{:S(2)}) collective-permute-start(bf16[32,160,64]{1,2,0:T(8,128)(2,1)} %collective-permute-done.10), channel_id=1, source_target_pairs={{0,1},{1,0},{2,3},{3,2},{4,5},{5,4},{6,7},{7,6},{8,9},{9,8},{10,11... | collective-permute-start | bytes 1966088 | tf_op jit(solution)/shard_map/ppermute | solution.py:31
  275.8 16.2 %copy-start.8 = (bf16[160,9,160]{2,0,1:T(8,128)(2,1)}, bf16[160,9,160]{2,0,1:T(8,128)(2,1)S(1)}, u32[]{:S(2)}) copy-start(bf16[160,9,160]{2,0,1:T(8,128)(2,1)S(1)} %collective-permute-done) | copy-start | bytes 1382404
  289.7 2.2 copy-start.9
  305.7 11.5 %copy-start.4 = (bf16[32,160,64]{1,2,0:T(8,128)(2,1)S(1)}, bf16[32,160,64]{1,2,0:T(8,128)(2,1)}, u32[]{:S(2)}) copy-start(bf16[32,160,64]{1,2,0:T(8,128)(2,1)} %param.10) | copy-start | bytes 1966084
  319.7 2.6 copy-start.2
  322.2 18.8 %all-to-all-start.2 = ((bf16[32,160,64]{1,2,0:T(8,128)(2,1)}), bf16[32,160,64]{1,2,0:T(8,128)(2,1)}, u32[]{:S(2)}, u32[]{:S(2)}) async-start(bf16[32,160,64]{1,2,0:T(8,128)(2,1)} %multiply_convert_fusion), calls=%async_computation.2 | async-start | bytes 2097152 | tf_op jit(solution)/shard_map/all_to_all | solution.py:176
  331.9 12.8 %copy-start.13 = (bf16[160,640]{1,0:T(8,128)(2,1)S(1)}, bf16[160,640]{1,0:T(8,128)(2,1)}, u32[]{:S(2)}) copy-start(bf16[160,640]{1,0:T(8,128)(2,1)} %param.15) | copy-start | bytes 614404
  331.9 19.7 %copy-start.20 = (s32[168]{0:T(256)S(1)}, s32[168]{0:T(256)}, u32[]{:S(2)}) copy-start(s32[168]{0:T(256)} %param.19) | copy-start | bytes 2020
  341.0 51.8 %all-to-all-start.1 = ((bf16[32,320,128]{2,1,0:T(8,128)(2,1)}), bf16[32,320,128]{2,1,0:T(8,128)(2,1)S(1)}, u32[]{:S(2)}, u32[]{:S(2)}) async-start(bf16[32,320,128]{2,1,0:T(8,128)(2,1)} %broadcast_select_fusion), calls=%async_computation.1 | async-start | bytes 5242880 | tf_op jit(solution)/shard_map/all_to_all | solution.py:177
  344.7 7.9 %collective-permute-start.15 = (bf16[160,640]{1,0:T(8,128)(2,1)S(1)}, bf16[160,640]{1,0:T(8,128)(2,1)S(1)}, u32[]{:S(2)}, u32[]{:S(2)}) collective-permute-start(bf16[160,640]{1,0:T(8,128)(2,1)S(1)} %copy-done.13), channel_id=1, source_target_pairs={{0,4},{4,8},{8,12},{12,0},{1,5},{5,9},{9,13},{13,1},{2,6},{6,10},{... | collective-permute-start | bytes 614408 | tf_op jit(solution)/shard_map/ppermute | solution.py:38
  344.7 18.7 %collective-permute-start.16 = (bf16[160,640]{1,0:T(8,128)(2,1)S(1)}, bf16[160,640]{1,0:T(8,128)(2,1)S(1)}, u32[]{:S(2)}, u32[]{:S(2)}) collective-permute-start(bf16[160,640]{1,0:T(8,128)(2,1)S(1)} %copy-done.13), channel_id=1, source_target_pairs={{0,8},{4,12},{8,0},{12,4},{1,9},{5,13},{9,1},{13,5},{2,10},{6,14},... | collective-permute-start | bytes 614408 | tf_op jit(solution)/shard_map/ppermute | solution.py:38
  346.8 27.7 %collective-permute-start.17 = (bf16[160,640]{1,0:T(8,128)(2,1)S(1)}, bf16[160,640]{1,0:T(8,128)(2,1)S(1)}, u32[]{:S(2)}, u32[]{:S(2)}) collective-permute-start(bf16[160,640]{1,0:T(8,128)(2,1)S(1)} %copy-done.13), channel_id=1, source_target_pairs={{0,12},{4,0},{8,4},{12,8},{1,13},{5,1},{9,5},{13,9},{2,14},{6,2},{... | collective-permute-start | bytes 614408 | tf_op jit(solution)/shard_map/ppermute | solution.py:38
  348.7 29.3 %collective-permute-start.12 = (bf16[160,640]{1,0:T(8,128)(2,1)}, bf16[160,640]{1,0:T(8,128)(2,1)}, u32[]{:S(2)}, u32[]{:S(2)}) collective-permute-start(bf16[160,640]{1,0:T(8,128)(2,1)} %param.16), channel_id=1, source_target_pairs={{0,4},{4,8},{8,12},{12,0},{1,5},{5,9},{9,13},{13,1},{2,6},{6,10},{... | collective-permute-start | bytes 614408 | tf_op jit(solution)/shard_map/ppermute | solution.py:38
  348.8 32.0 %collective-permute-start.13 = (bf16[160,640]{1,0:T(8,128)(2,1)}, bf16[160,640]{1,0:T(8,128)(2,1)}, u32[]{:S(2)}, u32[]{:S(2)}) collective-permute-start(bf16[160,640]{1,0:T(8,128)(2,1)} %param.16), channel_id=1, source_target_pairs={{0,8},{4,12},{8,0},{12,4},{1,9},{5,13},{9,1},{13,5},{2,10},{6,14},... | collective-permute-start | bytes 614408 | tf_op jit(solution)/shard_map/ppermute | solution.py:38
  352.6 21.9 %copy-start.14 = (bf16[160,640]{1,0:T(8,128)(2,1)}, bf16[160,640]{1,0:T(8,128)(2,1)S(1)}, u32[]{:S(2)}) copy-start(bf16[160,640]{1,0:T(8,128)(2,1)S(1)} %collective-permute-done.15) | copy-start | bytes 614404
  352.6 30.7 %collective-permute-start.14 = (bf16[160,640]{1,0:T(8,128)(2,1)}, bf16[160,640]{1,0:T(8,128)(2,1)}, u32[]{:S(2)}, u32[]{:S(2)}) collective-permute-start(bf16[160,640]{1,0:T(8,128)(2,1)} %param.16), channel_id=1, source_target_pairs={{0,12},{4,0},{8,4},{12,8},{1,13},{5,1},{9,5},{13,9},{2,14},{6,2},{... | collective-permute-start | bytes 614408 | tf_op jit(solution)/shard_map/ppermute | solution.py:38
  363.4 11.1 %copy-start.15 = (bf16[160,640]{1,0:T(8,128)(2,1)}, bf16[160,640]{1,0:T(8,128)(2,1)S(1)}, u32[]{:S(2)}) copy-start(bf16[160,640]{1,0:T(8,128)(2,1)S(1)} %collective-permute-done.16) | copy-start | bytes 614404
  374.5 0.7 copy-start.16
  393.0 1.7 copy-start.5
  428.4 7.1 %copy-start.1 = (bf16[42,320,128]{2,1,0:T(8,128)(2,1)S(1)}, bf16[42,320,128]{2,1,0:T(8,128)(2,1)}, u32[]{:S(2)}) copy-start(bf16[42,320,128]{2,1,0:T(8,128)(2,1)} %param.14) | copy-start | bytes 10321924
where the time goes:
time: 436 us; the launch traced here: 435 us
  waiting for transfers between devices  264 us (61%)
  local copies, waits for them, and re-layouts  50.8 us (12%)
  matrix products  41.8 us (10%)
  starting transfers between devices  33.2 us (8%)
  other arithmetic  32.2 us (7%)
  blocking collectives  13 us (3%)
    ppermute x12, waiting for transfers between devices, shift_parts(): lax.ppermute(shard, 'dp', [(i, (i + step) % count) for i in range(count)])  217 us
    ppermute x2, waiting for transfers between devices, pair_gather_channels(): across = lax.ppermute(field, 'mp', [(i, i ^ 2) for i in range(4)])  37.8 us
    dot_general x2, matrix products, apply_kernel(): jnp.einsum('scq,cte->steq', full_field, kernel, preferred_element_type=jn...  22.8 us
    gather x6, local copies, waits for them, and re-layouts, order_rows(): jnp.take(stacked, (my_shard - wanted_blocks) % count, axis=0, mode='clip')  20.6 us
    ppermute x12, starting transfers between devices, shift_parts(): lax.ppermute(shard, 'dp', [(i, (i + step) % count) for i in range(count)])  16.6 us
    all_to_all x1, blocking collectives, local(): lax.all_to_all(attended, 'mp', split_axis=1, concat_axis=0, tiled=True)  13 us
    dot_general x1, matrix products, local(): jnp.einsum('shqk,shdk->shdq', attention, value_heads, preferred_element_t...  11.1 us
    all_to_all x1, waiting for transfers between devices, local(): lax.all_to_all(normed_out, 'mp', split_axis=0, concat_axis=1, tiled=True)  9.13 us
  transfers between devices with their start and end apart: 21, of which 14 were waited for; matrix products, arithmetic and copies ran while one was open for 19% of the time, Pallas kernels for 0%

commit v1 on v0

--- a/solution.py
+++ b/solution.py
@@ -202,7 +202,10 @@
     attended = project(context.reshape(local_samples, total_width, cell_count), 3).astype(
         jnp.bfloat16
     )
-    returned = lax.all_to_all(attended, "mp", split_axis=1, concat_axis=0, tiled=True)
+    returned = jnp.concatenate(
+        lax.all_to_all(jnp.stack(jnp.split(attended, lax.axis_size("mp"), axis=1)), "mp", 0, 0),
+        axis=0,
+    )
     final_field = residual + returned.astype(jnp.float32)
     return final_field.astype(jnp.bfloat16)
 

time: 436 us -> 432 us (level)
  local copies, waits for them, and re-layouts: 50.8 us -> 43.5 us
  blocking collectives: 13 us -> 17.5 us
    convert_element_type x2 -> x0, local copies, waits for them, and re-layouts: 4.87 us -> none  [the longest x1 3.53 us: local(): final_field = residual + returned.astype(jnp.float32)]
    all_to_all x1, blocking collectives: 13 us -> 17.5 us  [local(): lax.all_to_all(jnp.stack(jnp.split(attended, lax.axis_size('mp'), axis=1)...]
where the time goes in v1:
time: 432 us; the launch traced here: 431 us
  waiting for transfers between devices  264 us (61%)
  local copies, waits for them, and re-layouts  43.5 us (10%)
  matrix products  41.8 us (10%)
  starting transfers between devices  33.2 us (8%)
  other arithmetic  30.3 us (7%)
  blocking collectives  17.5 us (4%)
    ppermute x12, waiting for transfers between devices, shift_parts(): lax.ppermute(shard, 'dp', [(i, (i + step) % count) for i in range(count)])  217 us
    ppermute x2, waiting for transfers between devices, pair_gather_channels(): across = lax.ppermute(field, 'mp', [(i, i ^ 2) for i in range(4)])  37.8 us
    dot_general x2, matrix products, apply_kernel(): jnp.einsum('scq,cte->steq', full_field, kernel, preferred_element_type=jn...  22.8 us
    gather x6, local copies, waits for them, and re-layouts, order_rows(): jnp.take(stacked, (my_shard - wanted_blocks) % count, axis=0, mode='clip')  20.6 us
    all_to_all x1, blocking collectives, local(): lax.all_to_all(jnp.stack(jnp.split(attended, lax.axis_size('mp'), axis=1)...  17.5 us
    ppermute x12, starting transfers between devices, shift_parts(): lax.ppermute(shard, 'dp', [(i, (i + step) % count) for i in range(count)])  16.6 us
    dot_general x1, matrix products, local(): jnp.einsum('shqk,shdk->shdq', attention, value_heads, preferred_element_t...  11.1 us
    all_to_all x1, waiting for transfers between devices, local(): lax.all_to_all(normed_out, 'mp', split_axis=0, concat_axis=1, tiled=True)  9.13 us
  transfers between devices with their start and end apart: 21, of which 14 were waited for; matrix products, arithmetic and copies ran while one was open for 19% of the time, Pallas kernels for 0%

profile of v1, /device:TPU:8, one launch (start us, length us, event | category | flops | bytes accessed | tf_op | source)
XLA Modules:
  0.0 430.9 jit_solution(8085982260813021998)
XLA Ops:
  2.3 3.5 gather_fusion.3
  5.8 5.5 %select_select_fusion = bf16[4,16,320,128]{3,2,1,0:T(8,128)(2,1)} fusion(bf16[4,16,320,128]{3,2,1,0:T(8,128)(2,1)} %bitcast.139, pred[4,16]{1,0:T(4,128)(4,1)S(1)} %compare_and_fusion, pred[4,16]{1,0:T(4,128)(4,1)S(1)} %broadcast_in_dim.133), kind=kLoop, calls=%fused_computation.25 | loop fusion | flops 5242880 | bytes 10485888 | tf_op jit(solution)/shard_map/jit(_where)/select_n | solution.py:115
  11.3 5.4 %all-to-all-start = ((bf16[4,16,320,128]{3,2,1,0:T(8,128)(2,1)}), bf16[4,16,320,128]{3,2,1,0:T(8,128)(2,1)}, u32[]{:S(2)}, u32[]{:S(2)}) async-start(bf16[4,16,320,128]{3,2,1,0:T(8,128)(2,1)} %select_select_fusion), calls=%async_computation | async-start | bytes 10485760 | tf_op jit(solution)/shard_map/all_to_all | solution.py:117
  23.9 2.0 collective-permute-start.5
  26.0 18.9 %collective-permute-done.7 = bf16[32,160,64]{1,2,0:T(8,128)(2,1)} collective-permute-done((bf16[32,160,64]{1,2,0:T(8,128)(2,1)}, bf16[32,160,64]{1,2,0:T(8,128)(2,1)}, u32[]{:S(2)}, u32[]{:S(2)}) %collective-permute-start.7) | collective-permute-done | bytes 655392 | tf_op jit(solution)/shard_map/ppermute | solution.py:29
  44.9 132.9 %collective-permute-done.3 = bf16[160,9,160]{2,0,1:T(8,128)(2,1)S(1)} collective-permute-done((bf16[160,9,160]{2,0,1:T(8,128)(2,1)S(1)}, bf16[160,9,160]{2,0,1:T(8,128)(2,1)S(1)}, u32[]{:S(2)}, u32[]{:S(2)}) %collective-permute-start.3) | collective-permute-done | bytes 460832 | tf_op jit(solution)/shard_map/ppermute | solution.py:38
  177.9 14.6 %collective-permute-done.4 = bf16[160,9,160]{2,0,1:T(8,128)(2,1)S(1)} collective-permute-done((bf16[160,9,160]{2,0,1:T(8,128)(2,1)S(1)}, bf16[160,9,160]{2,0,1:T(8,128)(2,1)S(1)}, u32[]{:S(2)}, u32[]{:S(2)}) %collective-permute-start.4) | collective-permute-done | bytes 460832 | tf_op jit(solution)/shard_map/ppermute | solution.py:38
  192.5 2.0 collective-permute-done.5
  195.4 2.2 pad_maximum_fusion.1
  197.6 2.4 gather_fusion.1
  200.0 6.2 %copy.35 = bf16[4,160,9,160]{1,0,3,2:T(4,128)(2,1)S(1)} copy(bf16[4,160,9,160]{3,1,2,0:T(8,128)(2,1)} %gather_fusion.1) | data formatting | bytes 3686400 | tf_op jit(solution)/shard_map/jit(_take)/gather | solution.py:45
  206.2 3.0 reshape.480
  209.2 11.4 %convolution_bitcast_fusion.1 = f32[32,9,160,8,8]{2,4,3,0,1:T(8,128)S(1)} fusion(bf16[32,160,64]{1,2,0:T(8,128)(2,1)} %collective-permute-done.8, bf16[32,160,64]{1,2,0:T(8,128)(2,1)} %collective-permute-done.7, bf16[32,160,64]{1,2,0:T(8,128)(2,1)} %collective-permute-done.6, bf16[32,160,64]{1,2,0:T(8,128)(2,1)} %fusion.36, ...), kind=kOutput, calls=%fused_computation.24 | convolution fusion | flops 3785359360 | bytes 16261120 | tf_op jit(solution)/shard_map/scq,cte->steq/dot_general | solution.py:60
  220.6 2.3 fusion.75
  224.1 1.7 multiply_convert_fusion.1
  227.4 1.7 collective-permute-start.1
  229.1 2.0 collective-permute-start.2
  231.5 18.9 %collective-permute-done.10 = bf16[32,160,64]{1,2,0:T(8,128)(2,1)} collective-permute-done((bf16[32,160,64]{1,2,0:T(8,128)(2,1)}, bf16[32,160,64]{1,2,0:T(8,128)(2,1)}, u32[]{:S(2)}, u32[]{:S(2)}) %collective-permute-start.10) | collective-permute-done | bytes 655392 | tf_op jit(solution)/shard_map/ppermute | solution.py:29
  250.7 25.1 %collective-permute-done = bf16[160,9,160]{2,0,1:T(8,128)(2,1)S(1)} collective-permute-done((bf16[160,9,160]{2,0,1:T(8,128)(2,1)S(1)}, bf16[160,9,160]{2,0,1:T(8,128)(2,1)S(1)}, u32[]{:S(2)}, u32[]{:S(2)}) %collective-permute-start) | collective-permute-done | bytes 460832 | tf_op jit(solution)/shard_map/ppermute | solution.py:38
  275.8 13.9 %collective-permute-done.1 = bf16[160,9,160]{2,0,1:T(8,128)(2,1)S(1)} collective-permute-done((bf16[160,9,160]{2,0,1:T(8,128)(2,1)S(1)}, bf16[160,9,160]{2,0,1:T(8,128)(2,1)S(1)}, u32[]{:S(2)}, u32[]{:S(2)}) %collective-permute-start.1) | collective-permute-done | bytes 460832 | tf_op jit(solution)/shard_map/ppermute | solution.py:38
  289.7 2.2 collective-permute-done.2
  292.0 2.2 pad_maximum_fusion
  294.1 2.4 gather_fusion
  296.6 6.2 %copy.34 = bf16[4,160,9,160]{1,0,3,2:T(4,128)(2,1)S(1)} copy(bf16[4,160,9,160]{3,1,2,0:T(8,128)(2,1)} %gather_fusion) | data formatting | bytes 3686400 | tf_op jit(solution)/shard_map/jit(_take)/gather | solution.py:45
  302.8 3.0 reshape.482
  305.7 11.5 %convolution_bitcast_fusion = f32[32,9,160,8,8]{2,4,3,0,1:T(8,128)S(1)} fusion(bf16[32,160,64]{1,2,0:T(8,128)(2,1)} %collective-permute-done.11, bf16[32,160,64]{1,2,0:T(8,128)(2,1)} %collective-permute-done.10, bf16[32,160,64]{1,2,0:T(8,128)(2,1)} %collective-permute-done.9, bf16[32,160,64]{1,2,0:T(8,128)(2,1)} %multiply_convert_fusion.1, ...), kind=kOutput, calls=%fused_computation.23 | convolution fusion | flops 3785359360 | bytes 16261120 | tf_op jit(solution)/shard_map/scq,cte->steq/dot_general | solution.py:60
  317.2 2.4 fusion.74
  322.2 4.3 all-to-all-start.2
  326.5 3.5 gather_fusion.4
  330.1 1.8 broadcast_select_fusion
  331.9 9.1 %all-to-all-done.2 = bf16[32,160,64]{1,2,0:T(8,128)(2,1)} async-done(((bf16[32,160,64]{1,2,0:T(8,128)(2,1)}), bf16[32,160,64]{1,2,0:T(8,128)(2,1)}, u32[]{:S(2)}, u32[]{:S(2)}) %all-to-all-start.2) | async-done | bytes 655392 | tf_op jit(solution)/shard_map/all_to_all | solution.py:176
  341.0 3.7 all-to-all-start.1
  344.7 2.0 collective-permute-start.16
  346.8 1.9 collective-permute-start.17
  348.8 2.7 collective-permute-start.13
  352.6 1.6 collective-permute-start.14
  354.3 9.2 %collective-permute-done.16 = bf16[160,640]{1,0:T(8,128)(2,1)S(1)} collective-permute-done((bf16[160,640]{1,0:T(8,128)(2,1)S(1)}, bf16[160,640]{1,0:T(8,128)(2,1)S(1)}, u32[]{:S(2)}, u32[]{:S(2)}) %collective-permute-start.16) | collective-permute-done | bytes 204832 | tf_op jit(solution)/shard_map/ppermute | solution.py:38
  363.4 11.0 %collective-permute-done.17 = bf16[160,640]{1,0:T(8,128)(2,1)S(1)} collective-permute-done((bf16[160,640]{1,0:T(8,128)(2,1)S(1)}, bf16[160,640]{1,0:T(8,128)(2,1)S(1)}, u32[]{:S(2)}, u32[]{:S(2)}) %collective-permute-start.17) | collective-permute-done | bytes 204832 | tf_op jit(solution)/shard_map/ppermute | solution.py:38
  378.0 2.8 collective-permute-done.13
  380.8 2.5 collective-permute-done.14
  383.3 2.2 pad_maximum_fusion.4
  385.5 1.8 gather_fusion.2
  387.4 3.1 fusion.50
  390.5 2.3 copy.41
  394.7 2.1 fusion.80
  396.8 1.9 fusion.79
  398.7 11.1 %convolution_convert_fusion = bf16[8,10,64,64]{3,2,1,0:T(8,128)(2,1)S(1)} fusion(bf16[8,10,64,128]{3,2,1,0:T(8,128)(2,1)} %bitcast.149, f32[8,10,64]{2,1,0:T(8,128)S(1)} %fusion.79, f32[8,10,64,128]{3,2,1,0:T(8,128)} %fusion.80, pred[8,128]{1,0:T(8,128)(4,1)S(1)} %iota_compare_fusion.4), kind=kOutput, calls=%fused_computation.87 | convolution fusion | flops 87495808 | bytes 4609024 | tf_op jit(solution)/shard_map/shqk,shdk->shdq/dot_general | solution.py:199
  411.9 17.5 %all_to_all.43 = bf16[4,8,160,64]{2,3,1,0:T(8,128)(2,1)S(1)} all-to-all(bf16[4,8,160,64]{2,3,1,0:T(8,128)(2,1)S(1)} %pad_maximum_fusion.2), channel_id=1, replica_groups=mesh['groups'=2,'dp'=4,'mp'=4] {'mp'}, dimensions={0} | all-to-all | bytes 1310720 | tf_op jit(solution)/shard_map/all_to_all | solution.py:206
  (140 shorter events, 26.3 us)
Async XLA Ops:
  0.0 2.3 copy-start
  11.3 5.5 %copy-start.4 = (bf16[32,160,64]{1,2,0:T(8,128)(2,1)S(1)}, bf16[32,160,64]{1,2,0:T(8,128)(2,1)}, u32[]{:S(2)}) copy-start(bf16[32,160,64]{1,2,0:T(8,128)(2,1)} %param.10) | copy-start | bytes 1966084
  11.3 310.9 %all-to-all-start = ((bf16[4,16,320,128]{3,2,1,0:T(8,128)(2,1)}), bf16[4,16,320,128]{3,2,1,0:T(8,128)(2,1)}, u32[]{:S(2)}, u32[]{:S(2)}) async-start(bf16[4,16,320,128]{3,2,1,0:T(8,128)(2,1)} %select_select_fusion), calls=%async_computation | async-start | bytes 10485760 | tf_op jit(solution)/shard_map/all_to_all | solution.py:117
  17.3 4.3 copy-start.7
  17.3 8.7 %copy-start.18 = (bf16[32,2,160]{2,1,0:T(2,128)(2,1)S(1)}, bf16[32,2,160]{2,1,0:T(2,128)(2,1)}, u32[]{:S(2)}) copy-start(bf16[32,2,160]{2,1,0:T(2,128)(2,1)} %param.11) | copy-start | bytes 61444
  19.9 25.0 %collective-permute-start.7 = (bf16[32,160,64]{1,2,0:T(8,128)(2,1)}, bf16[32,160,64]{1,2,0:T(8,128)(2,1)}, u32[]{:S(2)}, u32[]{:S(2)}) collective-permute-start(bf16[32,160,64]{1,2,0:T(8,128)(2,1)} %fusion.36), channel_id=1, source_target_pairs={{0,2},{1,3},{2,0},{3,1},{4,6},{5,7},{6,4},{7,5},{8,10},{9,11},{10,... | collective-permute-start | bytes 1966088 | tf_op jit(solution)/shard_map/ppermute | solution.py:29
  21.5 156.3 %collective-permute-start.3 = (bf16[160,9,160]{2,0,1:T(8,128)(2,1)S(1)}, bf16[160,9,160]{2,0,1:T(8,128)(2,1)S(1)}, u32[]{:S(2)}, u32[]{:S(2)}) collective-permute-start(bf16[160,9,160]{2,0,1:T(8,128)(2,1)S(1)} %copy-done.7), channel_id=1, source_target_pairs={{0,4},{4,8},{8,12},{12,0},{1,5},{5,9},{9,13},{13,1},{2,6},{6,10},{... | collective-permute-start | bytes 1382408 | tf_op jit(solution)/shard_map/ppermute | solution.py:38
  23.0 169.5 %collective-permute-start.4 = (bf16[160,9,160]{2,0,1:T(8,128)(2,1)S(1)}, bf16[160,9,160]{2,0,1:T(8,128)(2,1)S(1)}, u32[]{:S(2)}, u32[]{:S(2)}) collective-permute-start(bf16[160,9,160]{2,0,1:T(8,128)(2,1)S(1)} %copy-done.7), channel_id=1, source_target_pairs={{0,8},{4,12},{8,0},{12,4},{1,9},{5,13},{9,1},{13,5},{2,10},{6,14},... | collective-permute-start | bytes 1382408 | tf_op jit(solution)/shard_map/ppermute | solution.py:38
  23.9 170.6 %collective-permute-start.5 = (bf16[160,9,160]{2,0,1:T(8,128)(2,1)S(1)}, bf16[160,9,160]{2,0,1:T(8,128)(2,1)S(1)}, u32[]{:S(2)}, u32[]{:S(2)}) collective-permute-start(bf16[160,9,160]{2,0,1:T(8,128)(2,1)S(1)} %copy-done.7), channel_id=1, source_target_pairs={{0,12},{4,0},{8,4},{12,8},{1,13},{5,1},{9,5},{13,9},{2,14},{6,2},{... | collective-permute-start | bytes 1382408 | tf_op jit(solution)/shard_map/ppermute | solution.py:38
  25.9 183.3 %collective-permute-start.6 = (bf16[32,160,64]{1,2,0:T(8,128)(2,1)}, bf16[32,160,64]{1,2,0:T(8,128)(2,1)}, u32[]{:S(2)}, u32[]{:S(2)}) collective-permute-start(bf16[32,160,64]{1,2,0:T(8,128)(2,1)} %fusion.36), channel_id=1, source_target_pairs={{0,1},{1,0},{2,3},{3,2},{4,5},{5,4},{6,7},{7,6},{8,9},{9,8},{10,11... | collective-permute-start | bytes 1966088 | tf_op jit(solution)/shard_map/ppermute | solution.py:30
  44.9 164.3 %collective-permute-start.8 = (bf16[32,160,64]{1,2,0:T(8,128)(2,1)}, bf16[32,160,64]{1,2,0:T(8,128)(2,1)}, u32[]{:S(2)}, u32[]{:S(2)}) collective-permute-start(bf16[32,160,64]{1,2,0:T(8,128)(2,1)} %collective-permute-done.7), channel_id=1, source_target_pairs={{0,1},{1,0},{2,3},{3,2},{4,5},{5,4},{6,7},{7,6},{8,9},{9,8},{10,11... | collective-permute-start | bytes 1966088 | tf_op jit(solution)/shard_map/ppermute | solution.py:31
  177.8 16.7 %copy-start.11 = (bf16[160,9,160]{2,0,1:T(8,128)(2,1)}, bf16[160,9,160]{2,0,1:T(8,128)(2,1)S(1)}, u32[]{:S(2)}) copy-start(bf16[160,9,160]{2,0,1:T(8,128)(2,1)S(1)} %collective-permute-done.3) | copy-start | bytes 1382404
  192.5 2.1 copy-start.12
  194.5 0.9 copy-start.13
  223.7 3.7 copy-start.8
  223.7 7.4 %copy-start.19 = (s32[128]{0:T(128)S(1)}, s32[128]{0:T(128)}, u32[]{:S(2)}) copy-start(s32[128]{0:T(128)} %param.18) | copy-start | bytes 1540
  223.7 26.9 %copy-start.20 = (s32[128]{0:T(128)S(1)}, s32[128]{0:T(128)}, u32[]{:S(2)}) copy-start(s32[128]{0:T(128)} %param.17) | copy-start | bytes 1540
  225.9 24.5 %collective-permute-start.10 = (bf16[32,160,64]{1,2,0:T(8,128)(2,1)}, bf16[32,160,64]{1,2,0:T(8,128)(2,1)}, u32[]{:S(2)}, u32[]{:S(2)}) collective-permute-start(bf16[32,160,64]{1,2,0:T(8,128)(2,1)} %multiply_convert_fusion.1), channel_id=1, source_target_pairs={{0,2},{1,3},{2,0},{3,1},{4,6},{5,7},{6,4},{7,5},{8,10},{9,11},{10,... | collective-permute-start | bytes 1966088 | tf_op jit(solution)/shard_map/ppermute | solution.py:29
  227.4 48.4 %collective-permute-start = (bf16[160,9,160]{2,0,1:T(8,128)(2,1)S(1)}, bf16[160,9,160]{2,0,1:T(8,128)(2,1)S(1)}, u32[]{:S(2)}, u32[]{:S(2)}) collective-permute-start(bf16[160,9,160]{2,0,1:T(8,128)(2,1)S(1)} %copy-done.8), channel_id=1, source_target_pairs={{0,4},{4,8},{8,12},{12,0},{1,5},{5,9},{9,13},{13,1},{2,6},{6,10},{... | collective-permute-start | bytes 1382408 | tf_op jit(solution)/shard_map/ppermute | solution.py:38
  227.4 62.3 %collective-permute-start.1 = (bf16[160,9,160]{2,0,1:T(8,128)(2,1)S(1)}, bf16[160,9,160]{2,0,1:T(8,128)(2,1)S(1)}, u32[]{:S(2)}, u32[]{:S(2)}) collective-permute-start(bf16[160,9,160]{2,0,1:T(8,128)(2,1)S(1)} %copy-done.8), channel_id=1, source_target_pairs={{0,8},{4,12},{8,0},{12,4},{1,9},{5,13},{9,1},{13,5},{2,10},{6,14},... | collective-permute-start | bytes 1382408 | tf_op jit(solution)/shard_map/ppermute | solution.py:38
  229.1 62.9 %collective-permute-start.2 = (bf16[160,9,160]{2,0,1:T(8,128)(2,1)S(1)}, bf16[160,9,160]{2,0,1:T(8,128)(2,1)}, u32[]{:S(2)}, u32[]{:S(2)}) collective-permute-start(bf16[160,9,160]{2,0,1:T(8,128)(2,1)S(1)} %copy-done.8), channel_id=1, source_target_pairs={{0,12},{4,0},{8,4},{12,8},{1,13},{5,1},{9,5},{13,9},{2,14},{6,2},{... | collective-permute-start | bytes 1382408 | tf_op jit(solution)/shard_map/ppermute | solution.py:38
  231.4 74.4 %collective-permute-start.9 = (bf16[32,160,64]{1,2,0:T(8,128)(2,1)}, bf16[32,160,64]{1,2,0:T(8,128)(2,1)}, u32[]{:S(2)}, u32[]{:S(2)}) collective-permute-start(bf16[32,160,64]{1,2,0:T(8,128)(2,1)} %multiply_convert_fusion.1), channel_id=1, source_target_pairs={{0,1},{1,0},{2,3},{3,2},{4,5},{5,4},{6,7},{7,6},{8,9},{9,8},{10,11... | collective-permute-start | bytes 1966088 | tf_op jit(solution)/shard_map/ppermute | solution.py:30
  250.4 55.4 %collective-permute-start.11 = (bf16[32,160,64]{1,2,0:T(8,128)(2,1)}, bf16[32,160,64]{1,2,0:T(8,128)(2,1)}, u32[]{:S(2)}, u32[]{:S(2)}) collective-permute-start(bf16[32,160,64]{1,2,0:T(8,128)(2,1)} %collective-permute-done.10), channel_id=1, source_target_pairs={{0,1},{1,0},{2,3},{3,2},{4,5},{5,4},{6,7},{7,6},{8,9},{9,8},{10,11... | collective-permute-start | bytes 1966088 | tf_op jit(solution)/shard_map/ppermute | solution.py:31
  275.8 16.2 %copy-start.9 = (bf16[160,9,160]{2,0,1:T(8,128)(2,1)}, bf16[160,9,160]{2,0,1:T(8,128)(2,1)S(1)}, u32[]{:S(2)}) copy-start(bf16[160,9,160]{2,0,1:T(8,128)(2,1)S(1)} %collective-permute-done) | copy-start | bytes 1382404
  289.7 2.2 copy-start.10
  305.7 11.5 %copy-start.5 = (bf16[32,160,64]{1,2,0:T(8,128)(2,1)S(1)}, bf16[32,160,64]{1,2,0:T(8,128)(2,1)}, u32[]{:S(2)}) copy-start(bf16[32,160,64]{1,2,0:T(8,128)(2,1)} %param.10) | copy-start | bytes 1966084
  319.7 2.6 copy-start.2
  322.2 18.8 %all-to-all-start.2 = ((bf16[32,160,64]{1,2,0:T(8,128)(2,1)}), bf16[32,160,64]{1,2,0:T(8,128)(2,1)}, u32[]{:S(2)}, u32[]{:S(2)}) async-start(bf16[32,160,64]{1,2,0:T(8,128)(2,1)} %multiply_convert_fusion), calls=%async_computation.2 | async-start | bytes 2097152 | tf_op jit(solution)/shard_map/all_to_all | solution.py:176
  331.9 12.8 %copy-start.14 = (bf16[160,640]{1,0:T(8,128)(2,1)S(1)}, bf16[160,640]{1,0:T(8,128)(2,1)}, u32[]{:S(2)}) copy-start(bf16[160,640]{1,0:T(8,128)(2,1)} %param.15) | copy-start | bytes 614404
  331.9 19.7 %copy-start.21 = (s32[168]{0:T(256)S(1)}, s32[168]{0:T(256)}, u32[]{:S(2)}) copy-start(s32[168]{0:T(256)} %param.19) | copy-start | bytes 2020
  341.0 51.8 %all-to-all-start.1 = ((bf16[32,320,128]{2,1,0:T(8,128)(2,1)}), bf16[32,320,128]{2,1,0:T(8,128)(2,1)S(1)}, u32[]{:S(2)}, u32[]{:S(2)}) async-start(bf16[32,320,128]{2,1,0:T(8,128)(2,1)} %broadcast_select_fusion), calls=%async_computation.1 | async-start | bytes 5242880 | tf_op jit(solution)/shard_map/all_to_all | solution.py:177
  344.7 7.9 %collective-permute-start.15 = (bf16[160,640]{1,0:T(8,128)(2,1)S(1)}, bf16[160,640]{1,0:T(8,128)(2,1)S(1)}, u32[]{:S(2)}, u32[]{:S(2)}) collective-permute-start(bf16[160,640]{1,0:T(8,128)(2,1)S(1)} %copy-done.14), channel_id=1, source_target_pairs={{0,4},{4,8},{8,12},{12,0},{1,5},{5,9},{9,13},{13,1},{2,6},{6,10},{... | collective-permute-start | bytes 614408 | tf_op jit(solution)/shard_map/ppermute | solution.py:38
  344.7 18.7 %collective-permute-start.16 = (bf16[160,640]{1,0:T(8,128)(2,1)S(1)}, bf16[160,640]{1,0:T(8,128)(2,1)S(1)}, u32[]{:S(2)}, u32[]{:S(2)}) collective-permute-start(bf16[160,640]{1,0:T(8,128)(2,1)S(1)} %copy-done.14), channel_id=1, source_target_pairs={{0,8},{4,12},{8,0},{12,4},{1,9},{5,13},{9,1},{13,5},{2,10},{6,14},... | collective-permute-start | bytes 614408 | tf_op jit(solution)/shard_map/ppermute | solution.py:38
  346.8 27.7 %collective-permute-start.17 = (bf16[160,640]{1,0:T(8,128)(2,1)S(1)}, bf16[160,640]{1,0:T(8,128)(2,1)S(1)}, u32[]{:S(2)}, u32[]{:S(2)}) collective-permute-start(bf16[160,640]{1,0:T(8,128)(2,1)S(1)} %copy-done.14), channel_id=1, source_target_pairs={{0,12},{4,0},{8,4},{12,8},{1,13},{5,1},{9,5},{13,9},{2,14},{6,2},{... | collective-permute-start | bytes 614408 | tf_op jit(solution)/shard_map/ppermute | solution.py:38
  348.7 29.3 %collective-permute-start.12 = (bf16[160,640]{1,0:T(8,128)(2,1)}, bf16[160,640]{1,0:T(8,128)(2,1)}, u32[]{:S(2)}, u32[]{:S(2)}) collective-permute-start(bf16[160,640]{1,0:T(8,128)(2,1)} %param.16), channel_id=1, source_target_pairs={{0,4},{4,8},{8,12},{12,0},{1,5},{5,9},{9,13},{13,1},{2,6},{6,10},{... | collective-permute-start | bytes 614408 | tf_op jit(solution)/shard_map/ppermute | solution.py:38
  348.8 32.0 %collective-permute-start.13 = (bf16[160,640]{1,0:T(8,128)(2,1)}, bf16[160,640]{1,0:T(8,128)(2,1)}, u32[]{:S(2)}, u32[]{:S(2)}) collective-permute-start(bf16[160,640]{1,0:T(8,128)(2,1)} %param.16), channel_id=1, source_target_pairs={{0,8},{4,12},{8,0},{12,4},{1,9},{5,13},{9,1},{13,5},{2,10},{6,14},... | collective-permute-start | bytes 614408 | tf_op jit(solution)/shard_map/ppermute | solution.py:38
  352.6 21.9 %copy-start.15 = (bf16[160,640]{1,0:T(8,128)(2,1)}, bf16[160,640]{1,0:T(8,128)(2,1)S(1)}, u32[]{:S(2)}) copy-start(bf16[160,640]{1,0:T(8,128)(2,1)S(1)} %collective-permute-done.15) | copy-start | bytes 614404
  352.6 30.7 %collective-permute-start.14 = (bf16[160,640]{1,0:T(8,128)(2,1)}, bf16[160,640]{1,0:T(8,128)(2,1)}, u32[]{:S(2)}, u32[]{:S(2)}) collective-permute-start(bf16[160,640]{1,0:T(8,128)(2,1)} %param.16), channel_id=1, source_target_pairs={{0,12},{4,0},{8,4},{12,8},{1,13},{5,1},{9,5},{13,9},{2,14},{6,2},{... | collective-permute-start | bytes 614408 | tf_op jit(solution)/shard_map/ppermute | solution.py:38
  363.4 11.1 %copy-start.16 = (bf16[160,640]{1,0:T(8,128)(2,1)}, bf16[160,640]{1,0:T(8,128)(2,1)S(1)}, u32[]{:S(2)}) copy-start(bf16[160,640]{1,0:T(8,128)(2,1)S(1)} %collective-permute-done.16) | copy-start | bytes 614404
  374.5 0.7 copy-start.17
  393.0 1.7 copy-start.6
  411.7 17.7 %copy-start.3 = (f32[32,160,64]{1,2,0:T(8,128)S(1)}, f32[32,160,64]{1,2,0:T(8,128)}, u32[]{:S(2)}) copy-start(f32[32,160,64]{1,2,0:T(8,128)} %copy-done.2) | copy-start | bytes 3932164
  411.9 18.9 %copy-start.1 = (bf16[42,320,128]{2,1,0:T(8,128)(2,1)S(1)}, bf16[42,320,128]{2,1,0:T(8,128)(2,1)}, u32[]{:S(2)}) copy-start(bf16[42,320,128]{2,1,0:T(8,128)(2,1)} %param.14) | copy-start | bytes 10321924
